TPU v7x, 256 devices: a whole 4x4x8 slice. The times are simulated.
256 devices in a mesh: row: 16 (over z, y_hi), col: 16 (over x, y_lo, core).
Axes of the slice: x: 4, y: 4 (y_hi: 2, y_lo: 2; y = y_hi * 2 + y_lo), z: 8, core: 2. Of those that a mesh axis runs over, the one named last changes fastest.
Arguments:
- queries: bfloat16 [32, 2048, 128], P('row', 'col'), may hold values from -6.5 to 6.5
- keys: bfloat16 [32, 2048, 128], P('row', 'col'), may hold values from -6.5 to 6.5
- values: bfloat16 [32, 2048, 128], P('row', 'col'), may hold values from -6 to 6
- gate: bfloat16 [32, 2048, 128], P('row', 'col'), may hold values from -6 to 6
- bias: bfloat16 [4, 2048, 2048], P(None, 'col'), may hold values from -7.5 to 7.5
- grad_out: bfloat16 [32, 2048, 128], P('row', 'col'), may hold values from -6 to 6
- block_mask: int32 [16, 16], replicated, may hold values from 0 to 1, as said below
Outputs:
- query_grad: bfloat16 [32, 2048, 128], P('row', 'col')
- key_grad: bfloat16 [32, 2048, 128], P('row', 'col')
- value_grad: bfloat16 [32, 2048, 128], P('row', 'col')
- gate_grad: bfloat16 [32, 2048, 128], P('row', 'col')
- bias_grad: float32 [4, 2048, 2048], P(None, 'col', 'row')
Inputs may be any that keep to these rules, and one draw needn't show every extreme that they name: `block_mask`: every diagonal block is 1.
All inputs are finite; a program needn't handle non-finite values.
Results may differ from a plain program's by a relative error of at most 0.02.
Values may be sent and summed in bfloat16 or wider, within the bound.
No kernel may reach another device: no remote copies, remote signals or barrier semaphores. Data moves between devices by JAX's collectives and lax.ppermute only.
A program may use at most 64 MiB of HBM per device.

v0:
```python
import math
import jax
import jax.numpy as jnp
from jax import lax
from jax.sharding import PartitionSpec as P

H = 4
DH = 32
BLK = 128
NEGATIVE = -1000000000.0


def local(queries, keys, values, gate, bias, grad_out, block_mask):
    slab_rows, local_cols, channels = queries.shape
    head_count = H
    head_size = DH
    score_scale = 1.0 / math.sqrt(head_size)
    col_start = lax.axis_index("col") * local_cols
    kv_all = lax.all_gather(jnp.concatenate((keys, values), axis=2), "col", axis=1, tiled=True)
    key_all = kv_all[..., :channels]
    value_all = kv_all[..., channels:]
    all_cols = key_all.shape[1]
    query_heads = queries.reshape(slab_rows, local_cols, head_count, head_size)
    key_heads = key_all.reshape(slab_rows, all_cols, head_count, head_size)
    value_heads = value_all.reshape(slab_rows, all_cols, head_count, head_size)
    block_ids = (col_start + jnp.arange(local_cols, dtype=jnp.int32)) // BLK
    allowed = jnp.repeat(jnp.take(block_mask, block_ids, axis=0), BLK, axis=1) > 0
    products = jnp.einsum(
        "rjhd,rkhd->rhjk", query_heads, key_heads, preferred_element_type=jnp.float32
    )
    scores = products * score_scale + bias.astype(jnp.float32)[None]
    scores = jnp.where(allowed[None, None], scores, NEGATIVE)
    row_top = jnp.max(scores, axis=3, keepdims=True)
    log_total = row_top + jnp.log(jnp.sum(jnp.exp(scores - row_top), axis=3, keepdims=True))
    weights = jnp.exp(scores - log_total)
    probs = weights.astype(jnp.bfloat16)
    attended = jnp.einsum("rhjk,rkhd->rjhd", probs, value_heads, preferred_element_type=jnp.float32)
    gate_sig = jax.nn.sigmoid(gate.astype(jnp.float32)).reshape(
        slab_rows, local_cols, head_count, head_size
    )
    cotangent = grad_out.astype(jnp.float32).reshape(slab_rows, local_cols, head_count, head_size)
    gate_grad = (
        (cotangent * attended * gate_sig * (1.0 - gate_sig))
        .astype(jnp.bfloat16)
        .reshape(slab_rows, local_cols, channels)
    )
    out_grad = (cotangent * gate_sig).astype(jnp.bfloat16)
    grad_dot = jnp.transpose(jnp.sum(out_grad.astype(jnp.float32) * attended, axis=3), (0, 2, 1))
    prob_grad = jnp.einsum(
        "rjhd,rkhd->rhjk", out_grad, value_heads, preferred_element_type=jnp.float32
    )
    score_grad = weights * (prob_grad - grad_dot[..., None])
    score_grad_b = score_grad.astype(jnp.bfloat16)
    query_acc = jnp.einsum(
        "rhjk,rkhd->rjhd", score_grad_b, key_heads, preferred_element_type=jnp.float32
    )
    key_part = jnp.einsum(
        "rhjk,rjhd->rkhd", score_grad_b, query_heads, preferred_element_type=jnp.float32
    ).reshape(slab_rows, all_cols, channels)
    value_part = jnp.einsum(
        "rhjk,rjhd->rkhd", probs, out_grad, preferred_element_type=jnp.float32
    ).reshape(slab_rows, all_cols, channels)
    kv_part = jnp.concatenate((key_part, value_part), axis=2).astype(jnp.bfloat16)
    bias_part = jnp.sum(score_grad, axis=0).astype(jnp.bfloat16)
    col_count = all_cols // local_cols
    kv_moved = lax.all_to_all(
        kv_part.reshape(slab_rows, col_count, local_cols, 2 * channels), "col", 1, 1, tiled=True
    )
    kv_sum = jnp.sum(kv_moved.astype(jnp.float32), axis=1)
    key_grad = (kv_sum[..., :channels] * score_scale).astype(jnp.bfloat16)
    value_grad = kv_sum[..., channels:].astype(jnp.bfloat16)
    row_count = lax.axis_size("row")
    row_keys = all_cols // row_count
    bias_moved = lax.all_to_all(
        bias_part.reshape(head_count, local_cols, row_count, row_keys), "row", 2, 2, tiled=True
    )
    bias_grad = jnp.sum(bias_moved.astype(jnp.float32), axis=2)
    query_grad = (
        (query_acc * score_scale).astype(jnp.bfloat16).reshape(slab_rows, local_cols, channels)
    )
    return (query_grad, key_grad, value_grad, gate_grad, bias_grad)


def solution(mesh):
    return jax.shard_map(
        local,
        mesh=mesh,
        in_specs=(
            P("row", "col", None),
            P("row", "col", None),
            P("row", "col", None),
            P("row", "col", None),
            P(None, "col", None),
            P("row", "col", None),
            P(),
        ),
        out_specs=(
            P("row", "col", None),
            P("row", "col", None),
            P("row", "col", None),
            P("row", "col", None),
            P(None, "col", "row"),
        ),
        check_vma=False,
    )
```

profile of v0, /device:TPU:8, one launch (start us, length us, event | category | flops | bytes accessed | tf_op | source)
XLA Modules:
  0.0 172.1 jit_solution(1535113322949408808)
XLA Ops:
  7.2 0.0 copy-start
  7.2 0.0 copy-start.3
  7.2 0.0 all-gather.2.cloned.1.call-start
  7.2 1.5 pad_maximum_fusion.1
  8.8 0.0 all-gather.2.cloned.1.call-update
  8.8 0.9 copy.65
  9.8 0.9 add_divide_fusion
  10.6 0.1 copy.66
  10.7 4.1 %copy.64 = f32[4,128,2048]{1,2,0:T(8,128)} copy(bf16[4,128,2048]{2,1,0:T(8,128)(2,1)} %param.11) | data formatting | bytes 6291456 | tf_op jit(solution)/shard_map/convert_element_type | solution.py:31
  14.9 0.0 copy-done.3
  14.9 0.1 copy.63
  15.0 0.0 copy-done
  15.0 0.6 gather_fusion
  15.8 33.5 %all-gather.2.cloned.1.call-done = bf16[2,2048,256]{2,1,0:T(8,128)(2,1)} async-done(((bf16[2,128,256]{2,1,0:T(8,128)(2,1)}), bf16[2,2048,256]{2,1,0:T(8,128)(2,1)}) %all-gather.2.cloned.1.call-update) | async-done | bytes 2097168 | tf_op jit(solution)/shard_map/all_gather | solution.py:19
  49.3 1.7 fusion.15
  51.0 0.5 copy.61
  51.5 0.5 copy.67
  52.0 0.1 broadcast_in_dim.32
  52.1 4.5 %fusion.16 = (f32[2,4,128]{2,1,0:T(4,128)S(1)}, f32[2,4,128,2048]{2,3,1,0:T(8,128)S(1)}) fusion(f32[4,128,2048]{1,2,0:T(8,128)} %copy.64, bf16[2,2048,4,32]{1,3,2,0:T(8,128)(2,1)S(1)} %bitcast.49, bf16[2,128,4,32]{1,3,2,0:T(8,128)(2,1)S(1)} %bitcast.59, pred[128,2048]{0,1:T(8,128)(4,1)S(1)} %bitcast.58), kind=kOutput, calls=%fused_computation.42 | convolution fusion | flops 142605312 | bytes 13963264 | tf_op jit(solution)/shard_map/rjhd,rkhd->rhjk/dot_general | solution.py:28
  56.6 1.1 exponential_reduce_fusion
  57.7 1.7 %multiply_reduce_fusion = (f32[2,128,4]{1,2,0:T(4,128)S(1)}, bf16[2,128,4,32]{1,3,2,0:T(8,128)(2,1)S(1)}, bf16[2,128,4,32]{1,3,2,0:T(8,128)(2,1)S(1)}) fusion(f32[2,128,4,32]{1,3,2,0:T(8,128)S(1)} %bitcast.61, f32[2,128,4,32]{1,3,2,0:T(8,128)S(1)} %bitcast.62, bf16[2,2048,4,32]{1,3,2,0:T(8,128)(2,1)S(1)} %bitcast.51, ...), kind=kOutput, calls=%fused_computation.23 | convolution fusion | flops 138738688 | bytes 9838592 | tf_op jit(solution)/shard_map/rhjk,rkhd->rjhd/dot_general | solution.py:37
  59.5 1.5 convolution_convert_fusion
  61.0 5.0 %fusion.17 = (bf16[4,128,2048]{1,2,0:T(8,128)(2,1)}, bf16[2,4,128,2048]{2,3,1,0:T(8,128)(2,1)S(1)}) fusion(f32[2,4,128]{2,1,0:T(4,128)S(1)} %bitcast.70, bf16[2,128,4,32]{1,3,2,0:T(8,128)(2,1)S(1)} %get-tuple-element.26, bf16[2,2048,4,32]{1,3,2,0:T(8,128)(2,1)S(1)} %bitcast.52, f32[2,4,128,2048]{2,3,1,0:T(8,128)S(1)} %get-tuple-element.31, ...), kind=kOutput, calls=%fused_computation.43 | convolution fusion | flops 143654912 | bytes 15802368 | tf_op jit(solution)/shard_map/rjhd,rkhd->rhjk/dot_general | solution.py:49
  66.0 0.0 copy-start.1
  66.0 0.2 copy.88
  66.2 0.3 copy.74
  66.5 1.5 convolution_convert_fusion.1
  68.0 0.0 copy-done.1
  68.0 0.2 copy.87
  68.3 0.3 copy.73
  68.6 0.0 copy-start.2
  68.6 1.6 pad_maximum_fusion
  70.2 5.0 %all-to-all-start = ((bf16[2,16,128,256]{2,3,0,1:T(8,128)(2,1)}), bf16[2,16,128,256]{2,3,0,1:T(8,128)(2,1)}, u32[]{:S(2)}, u32[]{:S(2)}) async-start(bf16[2,16,128,256]{2,3,0,1:T(8,128)(2,1)} %pad_maximum_fusion), calls=%async_computation | async-start | bytes 4194304 | tf_op jit(solution)/shard_map/all_to_all | solution.py:66
  75.2 0.0 copy-done.2
  75.2 2.6 %copy.76 = bf16[4,128,16,128]{3,1,0,2:T(8,128)(2,1)} copy(bf16[4,128,16,128]{1,3,2,0:T(8,128)(2,1)S(1)} %bitcast.53) | data formatting | bytes 4194304 | tf_op jit(solution)/shard_map/convert_element_type | solution.py:64
  77.8 25.1 %all-to-all-done = bf16[2,16,128,256]{2,3,0,1:T(8,128)(2,1)} async-done(((bf16[2,16,128,256]{2,3,0,1:T(8,128)(2,1)}), bf16[2,16,128,256]{2,3,0,1:T(8,128)(2,1)}, u32[]{:S(2)}, u32[]{:S(2)}) %all-to-all-start) | async-done | bytes 2097184 | tf_op jit(solution)/shard_map/all_to_all | solution.py:66
  102.9 8.8 %all-to-all-start.1 = ((bf16[4,128,16,128]{3,1,0,2:T(8,128)(2,1)}), bf16[4,128,16,128]{3,1,0,2:T(8,128)(2,1)S(1)}, u32[]{:S(2)}, u32[]{:S(2)}) async-start(bf16[4,128,16,128]{3,1,0,2:T(8,128)(2,1)} %copy.76), calls=%async_computation.1 | async-start | bytes 4194304 | tf_op jit(solution)/shard_map/all_to_all | solution.py:74
  111.8 3.0 %fusion.8 = bf16[2,4,32,128]{3,2,1,0:T(8,128)(2,1)S(1)} fusion(bf16[2,2048,4,32]{1,3,2,0:T(8,128)(2,1)S(1)} %bitcast.50, bf16[2,4,128,2048]{2,3,1,0:T(8,128)(2,1)} %copy-done.1), kind=kOutput, calls=%fused_computation.17 | convolution fusion | flops 134283264 | bytes 5308416 | tf_op jit(solution)/shard_map/rhjk,rkhd->rjhd/dot_general | solution.py:54
  114.8 0.7 copy.77
  115.5 0.7 copy.80
  116.2 1.9 %convert_reduce_fusion.1 = f32[2,128,256]{1,2,0:T(8,128)S(1)} fusion(bf16[2,16,128,256]{2,3,0,1:T(8,128)(2,1)} %all-to-all-done), kind=kLoop, calls=%fused_computation.8 | loop fusion | flops 2031616 | bytes 2359296 | tf_op jit(solution)/shard_map/reduce_sum | solution.py:69
  118.2 0.7 copy.78
  118.9 0.7 copy.79
  119.7 44.5 %all-to-all-done.1 = bf16[4,128,16,128]{3,1,0,2:T(8,128)(2,1)S(1)} async-done(((bf16[4,128,16,128]{3,1,0,2:T(8,128)(2,1)}), bf16[4,128,16,128]{3,1,0,2:T(8,128)(2,1)S(1)}, u32[]{:S(2)}, u32[]{:S(2)}) %all-to-all-start.1) | async-done | bytes 2097184 | tf_op jit(solution)/shard_map/all_to_all | solution.py:74
  164.2 1.1 convert_reduce_fusion
  (8 shorter events, 0.1 us)
Async XLA Ops:
  7.2 7.9 %copy-start = (s32[16,16]{1,0:T(8,128)S(1)}, s32[16,16]{1,0:T(8,128)}, u32[]{:S(2)}) copy-start(s32[16,16]{1,0:T(8,128)} %param.13) | copy-start | bytes 3076
  7.2 7.7 %copy-start.3 = (bf16[2,128,128]{2,1,0:T(8,128)(2,1)S(1)}, bf16[2,128,128]{2,1,0:T(8,128)(2,1)}, u32[]{:S(2)}) copy-start(bf16[2,128,128]{2,1,0:T(8,128)(2,1)} %param.7) | copy-start | bytes 196612
  7.2 42.1 %all-gather.2.cloned.1.call-start = ((), (), s32[]{:S(2)}) async-start(), calls=%async_computation.2 | async-start | bytes 2228224 | tf_op jit(solution)/shard_map/all_gather | solution.py:19
  66.0 2.1 %copy-start.1 = (bf16[2,4,128,2048]{2,3,1,0:T(8,128)(2,1)}, bf16[2,4,128,2048]{2,3,1,0:T(8,128)(2,1)S(1)}, u32[]{:S(2)}) copy-start(bf16[2,4,128,2048]{2,3,1,0:T(8,128)(2,1)S(1)} %get-tuple-element.33) | copy-start | bytes 12582916
  68.6 6.6 %copy-start.2 = (bf16[4,128,2048]{1,2,0:T(8,128)(2,1)S(1)}, bf16[4,128,2048]{1,2,0:T(8,128)(2,1)}, u32[]{:S(2)}) copy-start(bf16[4,128,2048]{1,2,0:T(8,128)(2,1)} %get-tuple-element.32) | copy-start | bytes 6291460
  70.2 32.7 %all-to-all-start = ((bf16[2,16,128,256]{2,3,0,1:T(8,128)(2,1)}), bf16[2,16,128,256]{2,3,0,1:T(8,128)(2,1)}, u32[]{:S(2)}, u32[]{:S(2)}) async-start(bf16[2,16,128,256]{2,3,0,1:T(8,128)(2,1)} %pad_maximum_fusion), calls=%async_computation | async-start | bytes 4194304 | tf_op jit(solution)/shard_map/all_to_all | solution.py:66
  102.9 61.2 %all-to-all-start.1 = ((bf16[4,128,16,128]{3,1,0,2:T(8,128)(2,1)}), bf16[4,128,16,128]{3,1,0,2:T(8,128)(2,1)S(1)}, u32[]{:S(2)}, u32[]{:S(2)}) async-start(bf16[4,128,16,128]{3,1,0,2:T(8,128)(2,1)} %copy.76), calls=%async_computation.1 | async-start | bytes 4194304 | tf_op jit(solution)/shard_map/all_to_all | solution.py:74
Sparse Core Ops, SparseCore 0:
  10.4 38.8 all-gather.1
where the time goes:
time: 173 us; the launch traced here: 172 us
  waiting for transfers between devices  103 us (60%)
  matrix products  17.2 us (10%)
  local copies, waits for them, and re-layouts  15.4 us (9%)
  between operations  14.2 us (8%)
  starting transfers between devices  13.9 us (8%)
  other arithmetic  8.26 us (5%)
    all_to_all x1, waiting for transfers between devices, local(): lax.all_to_all(bias_part.reshape(head_count, local_cols, row_count, row_k...  44.5 us
    all_gather x1, waiting for transfers between devices, local(): lax.all_gather(jnp.concatenate((keys, values), axis=2), 'col', axis=1, ti...  33.5 us
    all_to_all x1, waiting for transfers between devices, local(): lax.all_to_all(kv_part.reshape(slab_rows, col_count, local_cols, 2 * chan...  25.1 us
    all_to_all x1, starting transfers between devices, local(): lax.all_to_all(bias_part.reshape(head_count, local_cols, row_count, row_k...  8.85 us
    all_to_all x1, starting transfers between devices, local(): lax.all_to_all(kv_part.reshape(slab_rows, col_count, local_cols, 2 * chan...  4.97 us
    dot_general x1, matrix products, local(): jnp.einsum('rjhd,rkhd->rhjk', out_grad, value_heads, preferred_element_ty...  4.96 us
    dot_general x1, matrix products, local(): jnp.einsum('rjhd,rkhd->rhjk', query_heads, key_heads, preferred_element_t...  4.46 us
    convert_element_type x1, local copies, waits for them, and re-layouts, local(): scores = products * score_scale + bias.astype(jnp.float32)[None]  4.13 us
  transfers between devices with their start and end apart: 3, of which 3 were waited for; matrix products, arithmetic and copies ran while one was open for 10% of the time, Pallas kernels for 0%

commit v1 on v0

--- a/solution.py
+++ b/solution.py
@@ -16,7 +16,10 @@
     head_size = DH
     score_scale = 1.0 / math.sqrt(head_size)
     col_start = lax.axis_index("col") * local_cols
-    kv_all = lax.all_gather(jnp.concatenate((keys, values), axis=2), "col", axis=1, tiled=True)
+    mine_x = jnp.concatenate((keys, values), axis=2)
+    kv_all = jnp.concatenate(
+        lax.all_to_all(jnp.stack([mine_x] * lax.axis_size("col"), 0), "col", 0, 0), 1
+    )
     key_all = kv_all[..., :channels]
     value_all = kv_all[..., channels:]
     all_cols = key_all.shape[1]

time: 173 us -> 157 us (0.908)
  between operations: 14.2 us -> 0.89 us
  waiting for transfers between devices: 103 us -> 91.9 us
  starting transfers between devices: 13.9 us -> 21 us
  local copies, waits for them, and re-layouts: 15.4 us -> 19.1 us
    all_gather x1 -> x0, waiting for transfers between devices: 33.5 us -> none  [local(): lax.all_gather(jnp.concatenate((keys, values), axis=2), 'col', axis=1, ti...]
    all_to_all x0 -> x1, waiting for transfers between devices: none -> 22.3 us  [local(): lax.all_to_all(jnp.stack([mine_x] * lax.axis_size('col'), 0), 'col', 0, 0)]
    all_to_all x0 -> x1, starting transfers between devices: none -> 5.77 us  [local(): lax.all_to_all(jnp.stack([mine_x] * lax.axis_size('col'), 0), 'col', 0, 0)]
    all_to_all x0 -> x1, local copies, waits for them, and re-layouts: none -> 2.6 us  [local(): lax.all_to_all(jnp.stack([mine_x] * lax.axis_size('col'), 0), 'col', 0, 0)]
    another operation x0 -> x1, local copies, waits for them, and re-layouts: none -> 1.81 us  [local(): jnp.stack([mine_x] * lax.axis_size('col'), 0)]
    unnamed x15 -> x19, local copies, waits for them, and re-layouts: 3.57 us -> 3.57 us
where the time goes in v1:
time: 157 us
  waiting for transfers between devices  91.9 us (59%)
  starting transfers between devices  21 us (13%)
  local copies, waits for them, and re-layouts  19.1 us (12%)
  matrix products  17.2 us (11%)
  other arithmetic  6.8 us (4%)
    all_to_all x1, waiting for transfers between devices, local(): lax.all_to_all(bias_part.reshape(head_count, local_cols, row_count, row_k...  44.5 us
    all_to_all x1, waiting for transfers between devices, local(): lax.all_to_all(kv_part.reshape(slab_rows, col_count, local_cols, 2 * chan...  25.1 us
    all_to_all x1, waiting for transfers between devices, local(): lax.all_to_all(jnp.stack([mine_x] * lax.axis_size('col'), 0), 'col', 0, 0)  22.3 us
    all_to_all x1, starting transfers between devices, local(): lax.all_to_all(bias_part.reshape(head_count, local_cols, row_count, row_k...  10.3 us
    all_to_all x1, starting transfers between devices, local(): lax.all_to_all(jnp.stack([mine_x] * lax.axis_size('col'), 0), 'col', 0, 0)  5.77 us
    all_to_all x1, starting transfers between devices, local(): lax.all_to_all(kv_part.reshape(slab_rows, col_count, local_cols, 2 * chan...  4.97 us
    dot_general x1, matrix products, local(): jnp.einsum('rjhd,rkhd->rhjk', out_grad, value_heads, preferred_element_ty...  4.97 us
    dot_general x1, matrix products, local(): jnp.einsum('rjhd,rkhd->rhjk', query_heads, key_heads, preferred_element_t...  4.46 us
  transfers between devices with their start and end apart: 3, of which 3 were waited for; matrix products, arithmetic and copies ran while one was open for 10% of the time, Pallas kernels for 0%

profile of v1, /device:TPU:8, one launch (start us, length us, event | category | flops | bytes accessed | tf_op | source)
XLA Modules:
  0.0 157.0 jit_solution(14494070827637920644)
XLA Ops:
  0.6 0.0 copy-start
  0.6 0.0 copy-start.3
  0.7 0.0 copy-start.4
  0.7 0.9 pad_maximum_fusion.1
  1.6 0.1 copy.80
  1.7 1.8 %stack.2 = bf16[16,2,128,256]{2,3,1,0:T(8,128)(2,1)} broadcast(bf16[2,128,256]{1,2,0:T(8,128)(2,1)S(1)} %copy.80), dimensions={1,2,3} | broadcast | bytes 2228224 | tf_op jit(solution)/shard_map/stack | solution.py:21
  3.5 5.8 %all-to-all-start = ((bf16[16,2,128,256]{2,3,1,0:T(8,128)(2,1)}), bf16[16,2,128,256]{2,3,1,0:T(8,128)(2,1)S(1)}, u32[]{:S(2)}, u32[]{:S(2)}) async-start(bf16[16,2,128,256]{2,3,1,0:T(8,128)(2,1)} %stack.2), calls=%async_computation | async-start | bytes 4194304 | tf_op jit(solution)/shard_map/all_to_all | solution.py:21
  9.3 0.0 copy-start.5
  9.3 0.0 copy-done.3
  9.3 0.1 copy.86
  9.4 0.0 copy-done.4
  9.5 0.1 copy.87
  9.6 4.1 %copy.85 = f32[4,128,2048]{1,2,0:T(8,128)} copy(bf16[4,128,2048]{2,1,0:T(8,128)(2,1)} %param.11) | data formatting | bytes 6291456 | tf_op jit(solution)/shard_map/convert_element_type | solution.py:34
  13.7 0.0 copy-done.5
  13.7 0.1 copy.84
  13.9 0.0 copy-done
  13.9 0.6 gather_fusion
  14.6 22.3 %all-to-all-done = bf16[16,2,128,256]{2,3,1,0:T(8,128)(2,1)S(1)} async-done(((bf16[16,2,128,256]{2,3,1,0:T(8,128)(2,1)}), bf16[16,2,128,256]{2,3,1,0:T(8,128)(2,1)S(1)}, u32[]{:S(2)}, u32[]{:S(2)}) %all-to-all-start) | async-done | bytes 2097184 | tf_op jit(solution)/shard_map/all_to_all | solution.py:21
  36.9 2.6 %copy.81 = bf16[16,2,128,256]{3,2,0,1:T(8,128)(2,1)} copy(bf16[16,2,128,256]{2,3,1,0:T(8,128)(2,1)S(1)} %all-to-all-done) | data formatting | bytes 4194304 | tf_op jit(solution)/shard_map/all_to_all | solution.py:21
  39.6 1.7 %fusion.15 = (bf16[2,2048,128]{2,1,0:T(8,128)(2,1)S(1)}, bf16[2,2048,128]{2,1,0:T(8,128)(2,1)S(1)}) fusion(bf16[2,2048,256]{2,1,0:T(8,128)(2,1)} %bitcast.57), kind=kLoop, calls=%fused_computation.41 | loop fusion | bytes 4194304 | tf_op jit(solution)/shard_map/slice | solution.py:24
  41.3 0.5 copy.82
  41.8 0.5 copy.88
  42.3 0.1 broadcast_in_dim.32
  42.4 4.5 %fusion.16 = (f32[2,4,128]{2,1,0:T(4,128)S(1)}, f32[2,4,128,2048]{2,3,1,0:T(8,128)S(1)}) fusion(f32[4,128,2048]{1,2,0:T(8,128)} %copy.85, bf16[2,2048,4,32]{1,3,2,0:T(8,128)(2,1)S(1)} %bitcast.52, bf16[2,128,4,32]{1,3,2,0:T(8,128)(2,1)S(1)} %bitcast.63, pred[128,2048]{0,1:T(8,128)(4,1)S(1)} %bitcast.62), kind=kOutput, calls=%fused_computation.42 | convolution fusion | flops 142605312 | bytes 13963264 | tf_op jit(solution)/shard_map/rjhd,rkhd->rhjk/dot_general | solution.py:31
  46.9 1.1 exponential_reduce_fusion
  48.0 1.7 %multiply_reduce_fusion = (f32[2,128,4]{1,2,0:T(4,128)S(1)}, bf16[2,128,4,32]{1,3,2,0:T(8,128)(2,1)S(1)}, bf16[2,128,4,32]{1,3,2,0:T(8,128)(2,1)S(1)}) fusion(f32[2,128,4,32]{1,3,2,0:T(8,128)S(1)} %bitcast.65, f32[2,128,4,32]{1,3,2,0:T(8,128)S(1)} %bitcast.66, bf16[2,2048,4,32]{1,3,2,0:T(8,128)(2,1)S(1)} %bitcast.54, ...), kind=kOutput, calls=%fused_computation.23 | convolution fusion | flops 138738688 | bytes 9838592 | tf_op jit(solution)/shard_map/rhjk,rkhd->rjhd/dot_general | solution.py:40
  49.8 1.5 convolution_convert_fusion
  51.3 5.0 %fusion.17 = (bf16[4,128,2048]{1,2,0:T(8,128)(2,1)}, bf16[2,4,128,2048]{2,3,1,0:T(8,128)(2,1)S(1)}) fusion(f32[2,4,128]{2,1,0:T(4,128)S(1)} %bitcast.74, bf16[2,128,4,32]{1,3,2,0:T(8,128)(2,1)S(1)} %get-tuple-element.31, bf16[2,2048,4,32]{1,3,2,0:T(8,128)(2,1)S(1)} %bitcast.55, f32[2,4,128,2048]{2,3,1,0:T(8,128)S(1)} %get-tuple-element.36, ...), kind=kOutput, calls=%fused_computation.43 | convolution fusion | flops 143654912 | bytes 15802368 | tf_op jit(solution)/shard_map/rjhd,rkhd->rhjk/dot_general | solution.py:52
  56.3 0.0 copy-start.1
  56.3 0.2 copy.109
  56.5 0.3 copy.95
  56.8 1.5 convolution_convert_fusion.1
  58.3 0.0 copy-done.1
  58.3 0.2 copy.108
  58.6 0.3 copy.94
  58.8 0.0 copy-start.2
  58.9 1.6 %pad_maximum_fusion = bf16[2,16,128,256]{2,3,0,1:T(8,128)(2,1)} fusion(bf16[2,16,128,128]{2,3,0,1:T(8,128)(2,1)S(1)} %copy.95, bf16[2,16,128,128]{2,3,0,1:T(8,128)(2,1)S(1)} %copy.94), kind=kLoop, calls=%fused_computation.11 | loop fusion | flops 4194304 | bytes 4194304 | tf_op jit(solution)/shard_map/concatenate | solution.py:66
  60.5 5.0 %all-to-all-start.1 = ((bf16[2,16,128,256]{2,3,0,1:T(8,128)(2,1)}), bf16[2,16,128,256]{2,3,0,1:T(8,128)(2,1)}, u32[]{:S(2)}, u32[]{:S(2)}) async-start(bf16[2,16,128,256]{2,3,0,1:T(8,128)(2,1)} %pad_maximum_fusion), calls=%async_computation.1 | async-start | bytes 4194304 | tf_op jit(solution)/shard_map/all_to_all | solution.py:69
  65.4 0.0 copy-done.2
  65.5 2.6 %copy.97 = bf16[4,128,16,128]{3,1,0,2:T(8,128)(2,1)} copy(bf16[4,128,16,128]{1,3,2,0:T(8,128)(2,1)S(1)} %bitcast.56) | data formatting | bytes 4194304 | tf_op jit(solution)/shard_map/convert_element_type | solution.py:67
  68.1 25.1 %all-to-all-done.1 = bf16[2,16,128,256]{2,3,0,1:T(8,128)(2,1)} async-done(((bf16[2,16,128,256]{2,3,0,1:T(8,128)(2,1)}), bf16[2,16,128,256]{2,3,0,1:T(8,128)(2,1)}, u32[]{:S(2)}, u32[]{:S(2)}) %all-to-all-start.1) | async-done | bytes 2097184 | tf_op jit(solution)/shard_map/all_to_all | solution.py:69
  93.2 10.3 %all-to-all-start.2 = ((bf16[4,128,16,128]{3,1,0,2:T(8,128)(2,1)}), bf16[4,128,16,128]{3,1,0,2:T(8,128)(2,1)S(1)}, u32[]{:S(2)}, u32[]{:S(2)}) async-start(bf16[4,128,16,128]{3,1,0,2:T(8,128)(2,1)} %copy.97), calls=%async_computation.2 | async-start | bytes 4194304 | tf_op jit(solution)/shard_map/all_to_all | solution.py:77
  103.5 3.0 %fusion.8 = bf16[2,4,32,128]{3,2,1,0:T(8,128)(2,1)S(1)} fusion(bf16[2,2048,4,32]{1,3,2,0:T(8,128)(2,1)S(1)} %bitcast.53, bf16[2,4,128,2048]{2,3,1,0:T(8,128)(2,1)} %copy-done.1), kind=kOutput, calls=%fused_computation.17 | convolution fusion | flops 134283264 | bytes 5308416 | tf_op jit(solution)/shard_map/rhjk,rkhd->rjhd/dot_general | solution.py:57
  106.5 0.7 copy.98
  107.2 0.7 copy.101
  108.0 1.9 %convert_reduce_fusion.1 = f32[2,128,256]{1,2,0:T(8,128)S(1)} fusion(bf16[2,16,128,256]{2,3,0,1:T(8,128)(2,1)} %all-to-all-done.1), kind=kLoop, calls=%fused_computation.8 | loop fusion | flops 2031616 | bytes 2359296 | tf_op jit(solution)/shard_map/reduce_sum | solution.py:72
  109.9 0.7 copy.99
  110.7 0.7 copy.100
  111.4 44.5 %all-to-all-done.2 = bf16[4,128,16,128]{3,1,0,2:T(8,128)(2,1)S(1)} async-done(((bf16[4,128,16,128]{3,1,0,2:T(8,128)(2,1)}), bf16[4,128,16,128]{3,1,0,2:T(8,128)(2,1)S(1)}, u32[]{:S(2)}, u32[]{:S(2)}) %all-to-all-start.2) | async-done | bytes 2097184 | tf_op jit(solution)/shard_map/all_to_all | solution.py:77
  155.9 1.1 convert_reduce_fusion
  (9 shorter events, 0.2 us)
Async XLA Ops:
  0.6 13.3 %copy-start = (s32[16,16]{1,0:T(8,128)S(1)}, s32[16,16]{1,0:T(8,128)}, u32[]{:S(2)}) copy-start(s32[16,16]{1,0:T(8,128)} %param.13) | copy-start | bytes 3076
  0.6 8.7 %copy-start.3 = (bf16[2,128,128]{2,1,0:T(8,128)(2,1)S(1)}, bf16[2,128,128]{2,1,0:T(8,128)(2,1)}, u32[]{:S(2)}) copy-start(bf16[2,128,128]{2,1,0:T(8,128)(2,1)} %param.12) | copy-start | bytes 196612
  0.7 8.8 %copy-start.4 = (bf16[2,128,128]{2,1,0:T(8,128)(2,1)S(1)}, bf16[2,128,128]{2,1,0:T(8,128)(2,1)}, u32[]{:S(2)}) copy-start(bf16[2,128,128]{2,1,0:T(8,128)(2,1)} %param.10) | copy-start | bytes 196612
  3.5 33.4 %all-to-all-start = ((bf16[16,2,128,256]{2,3,1,0:T(8,128)(2,1)}), bf16[16,2,128,256]{2,3,1,0:T(8,128)(2,1)S(1)}, u32[]{:S(2)}, u32[]{:S(2)}) async-start(bf16[16,2,128,256]{2,3,1,0:T(8,128)(2,1)} %stack.2), calls=%async_computation | async-start | bytes 4194304 | tf_op jit(solution)/shard_map/all_to_all | solution.py:21
  9.3 4.4 %copy-start.5 = (bf16[2,128,128]{2,1,0:T(8,128)(2,1)S(1)}, bf16[2,128,128]{2,1,0:T(8,128)(2,1)}, u32[]{:S(2)}) copy-start(bf16[2,128,128]{2,1,0:T(8,128)(2,1)} %param.7) | copy-start | bytes 196612
  56.3 2.1 %copy-start.1 = (bf16[2,4,128,2048]{2,3,1,0:T(8,128)(2,1)}, bf16[2,4,128,2048]{2,3,1,0:T(8,128)(2,1)S(1)}, u32[]{:S(2)}) copy-start(bf16[2,4,128,2048]{2,3,1,0:T(8,128)(2,1)S(1)} %get-tuple-element.38) | copy-start | bytes 12582916
  58.8 6.6 %copy-start.2 = (bf16[4,128,2048]{1,2,0:T(8,128)(2,1)S(1)}, bf16[4,128,2048]{1,2,0:T(8,128)(2,1)}, u32[]{:S(2)}) copy-start(bf16[4,128,2048]{1,2,0:T(8,128)(2,1)} %get-tuple-element.37) | copy-start | bytes 6291460
  60.5 32.7 %all-to-all-start.1 = ((bf16[2,16,128,256]{2,3,0,1:T(8,128)(2,1)}), bf16[2,16,128,256]{2,3,0,1:T(8,128)(2,1)}, u32[]{:S(2)}, u32[]{:S(2)}) async-start(bf16[2,16,128,256]{2,3,0,1:T(8,128)(2,1)} %pad_maximum_fusion), calls=%async_computation.1 | async-start | bytes 4194304 | tf_op jit(solution)/shard_map/all_to_all | solution.py:69
  93.2 62.7 %all-to-all-start.2 = ((bf16[4,128,16,128]{3,1,0,2:T(8,128)(2,1)}), bf16[4,128,16,128]{3,1,0,2:T(8,128)(2,1)S(1)}, u32[]{:S(2)}, u32[]{:S(2)}) async-start(bf16[4,128,16,128]{3,1,0,2:T(8,128)(2,1)} %copy.97), calls=%async_computation.2 | async-start | bytes 4194304 | tf_op jit(solution)/shard_map/all_to_all | solution.py:77
